TPU v7x, 32 devices: a whole 2x2x4 slice. The times are simulated.
32 devices in a mesh: row: 4 (over z), col: 4 (over y, x), walk: 2 (over core).
Axes of the slice: x: 2, y: 2, z: 4, core: 2. Of those that a mesh axis runs over, the one named last changes fastest.
Arguments:
- one_elec: bfloat16 [8, 512, 256], P('walk', ('row', 'col')), parts along dimension 0, may hold values from -13 to 13
- pair: bfloat16 [8, 512, 512, 128], P('walk', 'row', 'col'), parts along dimension 0, may hold values from -11 to 11
- spins: int32 [512], replicated, may hold values from 0 to 1, as said below
- w_single: bfloat16 [1024, 256], replicated, may hold values from -0.1875 to 0.1875
- b_single: float32 [256], replicated, may hold values from -1 to 1
- w_pair: bfloat16 [128, 128], replicated, may hold values from -0.5 to 0.5
- w_msg: bfloat16 [256, 128], replicated, may hold values from -0.375 to 0.375
- b_pair: float32 [128], replicated, may hold values from -1 to 1
- d_single: bfloat16 [8, 512, 256], P('walk', ('row', 'col')), parts along dimension 0, may hold values from -13 to 13
- d_pair: bfloat16 [8, 512, 512, 128], P('walk', 'row', 'col'), parts along dimension 0, may hold values from -6 to 6
Outputs:
- single_out: bfloat16 [8, 512, 256], P('walk', ('row', 'col')), parts along dimension 0
- pair_out: bfloat16 [8, 512, 512, 128], P('walk', 'row', 'col'), parts along dimension 0
- grad_single: float32 [8, 512, 256], P('walk', ('row', 'col')), parts along dimension 0
- grad_pair: bfloat16 [8, 512, 512, 128], P('walk', 'row', 'col'), parts along dimension 0
There are 2 independent parts, one for each index of `walk`. A program takes and returns all parts, laid end to end along the dimension named above; an argument that names none is the same for every part. Nothing has to cross between parts.
Inputs may be any that keep to these rules, and one draw needn't show every extreme that they name: `spins`: 1 marks a spin-up electron and 0 a spin-down one; from 128 to 384 electrons are up.
All inputs are finite; a program needn't handle non-finite values.
Results may differ from a plain program's by a relative error of at most 0.005.
Values may be sent and summed in bfloat16 or wider, within the bound.
No kernel may reach another device: no remote copies, remote signals or barrier semaphores. Data moves between devices by JAX's collectives and lax.ppermute only.
A program may use at most 192 MiB of HBM per device.

v0:
```python
import jax
import jax.numpy as jnp
from jax import lax
from jax.sharding import PartitionSpec as P

highest = lax.Precision.HIGHEST


def from_root(value, axis, source):
    kept = jnp.where(lax.axis_index(axis) == source, value, 0).astype(value.dtype)
    return lax.psum(kept, axis)


def body(one_elec, pair, spins, w_single, b_single, w_pair, w_msg, b_pair, d_single, d_pair):
    walkers, block_rows, block_cols, width_pair = pair.shape
    own_rows = one_elec.shape[1]
    width_single = one_elec.shape[2]
    electrons = spins.shape[0]
    pair_down = float(electrons) ** (-0.75)
    pair_boost = float(electrons) ** 0.75
    row_index = lax.axis_index("row")
    col_index = lax.axis_index("col")
    spin_up = spins.astype(jnp.float32)
    spin_down = 1.0 - spin_up
    count_up = jnp.sum(spin_up)
    count_down = jnp.sum(spin_down)
    counts = jnp.stack([count_up, count_down])
    spin_table = jnp.stack([spin_up, spin_down], axis=1)
    col_start = col_index * block_cols
    own_start = (row_index * lax.axis_size("col") + col_index) * own_rows
    col_table = lax.dynamic_slice_in_dim(spin_table, col_start, block_cols, 0)
    own_table = lax.dynamic_slice_in_dim(spin_table, own_start, own_rows, 0)
    everyone = lax.all_gather(one_elec, ("row", "col"), axis=1, tiled=True)
    spin_sums = jnp.einsum(
        "wjd,js->wsd", everyone, spin_table.astype(jnp.bfloat16), preferred_element_type=jnp.float32
    )
    col_single = lax.dynamic_slice_in_dim(everyone, col_start, block_cols, 1)
    spin_means = spin_sums / counts[None, :, None]
    partial_value = jnp.einsum(
        "wijd,js->wisd", pair, col_table.astype(jnp.bfloat16), preferred_element_type=jnp.float32
    )
    summed_pair = lax.psum(partial_value.astype(jnp.bfloat16), "col").astype(jnp.float32)
    own_sum = lax.dynamic_slice_in_dim(summed_pair, col_index * own_rows, own_rows, 1)
    pair_means = own_sum / counts[None, None, :, None]
    single_wide = one_elec.astype(jnp.float32)
    features = jnp.concatenate(
        [
            single_wide,
            jnp.broadcast_to(spin_means[:, None, 0, :], (walkers, own_rows, width_single)),
            jnp.broadcast_to(spin_means[:, None, 1, :], (walkers, own_rows, width_single)),
            pair_means[:, :, 0, :],
            pair_means[:, :, 1, :],
        ],
        axis=2,
    ).astype(jnp.bfloat16)
    single_act = jnp.tanh(
        jnp.einsum("wif,fd->wid", features, w_single, preferred_element_type=jnp.float32) + b_single
    )
    single_out = (single_wide + single_act).astype(jnp.bfloat16)
    message = jnp.einsum("wjd,de->wje", col_single, w_msg, preferred_element_type=jnp.float32)
    pre_pair = (
        jnp.einsum("wijd,de->wije", pair, w_pair, preferred_element_type=jnp.float32)
        + message[:, None, :, :]
        + b_pair
    )
    pair_act = jnp.tanh(pre_pair)
    pair_out = (pair.astype(jnp.float32) + pair_act).astype(jnp.bfloat16)
    grad_pre = (d_single.astype(jnp.float32) * (1.0 - single_act * single_act)).astype(jnp.bfloat16)
    feature_grad = jnp.einsum("wid,fd->wif", grad_pre, w_single, preferred_element_type=jnp.float32)
    grad_direct = feature_grad[:, :, :width_single]
    grad_means = feature_grad[:, :, width_single : 3 * width_single].reshape(
        walkers, own_rows, 2, width_single
    )
    grad_pair_means = feature_grad[:, :, 3 * width_single :].reshape(
        walkers, own_rows, 2, width_pair
    )
    row_pair_grads = lax.all_gather(
        grad_pair_means.astype(jnp.bfloat16), "col", axis=1, tiled=True
    ).astype(grad_pair_means.dtype)
    col_up = col_table[:, 0]
    col_down = col_table[:, 1]
    spread_pair = (
        col_up[None, None, :, None] * (row_pair_grads[:, :, 0, :] / count_up)[:, :, None, :]
        + col_down[None, None, :, None] * (row_pair_grads[:, :, 1, :] / count_down)[:, :, None, :]
    )
    pair_delta = (d_pair.astype(jnp.float32) * (1.0 - pair_act * pair_act)).astype(jnp.bfloat16)
    back_pair = jnp.einsum("wije,de->wijd", pair_delta, w_pair, preferred_element_type=jnp.float32)
    grad_pair = (d_pair.astype(jnp.float32) + back_pair + pair_boost * spread_pair).astype(
        jnp.bfloat16
    )
    column_sum = jnp.sum(pair_delta, axis=1, dtype=jnp.float32)
    message_grad = pair_down * jnp.einsum(
        "wje,de->wjd", column_sum, w_msg.astype(jnp.float32), precision=highest
    )
    mean_sums = jnp.sum(grad_means, axis=1)
    column_total = lax.psum(message_grad.astype(jnp.bfloat16), "row").astype(jnp.float32)
    row_total = from_root(column_total.astype(jnp.bfloat16), "col", row_index).astype(
        column_total.dtype
    )
    own_message = lax.dynamic_slice_in_dim(row_total, col_index * own_rows, own_rows, 1)
    mean_total = lax.psum(mean_sums, ("row", "col"))
    own_up = own_table[:, 0]
    own_down = own_table[:, 1]
    electron_grad = (
        own_up[None, :, None] * (mean_total[:, 0, :] / count_up)[:, None, :]
        + own_down[None, :, None] * (mean_total[:, 1, :] / count_down)[:, None, :]
        + own_message
    )
    grad_single = d_single.astype(jnp.float32) + grad_direct + electron_grad
    return (single_out, pair_out, grad_single, grad_pair)


def solution(mesh):
    placed = (
        P("walk", ("row", "col"), None),
        P("walk", "row", "col", None),
        P(),
        P(),
        P(),
        P(),
        P(),
        P(),
        P("walk", ("row", "col"), None),
        P("walk", "row", "col", None),
    )
    return jax.shard_map(
        body,
        mesh=mesh,
        in_specs=placed,
        out_specs=(
            P("walk", ("row", "col"), None),
            P("walk", "row", "col", None),
            P("walk", ("row", "col"), None),
            P("walk", "row", "col", None),
        ),
        check_vma=False,
    )
```

profile of v0, /device:TPU:0, one launch (start us, length us, event | category | flops | bytes accessed | tf_op | source)
XLA Modules:
  0.0 284.7 jit_solution(3167523664300797299)
XLA Ops:
  7.2 0.0 copy-start
  7.2 0.0 all-gather.2.cloned.1.call-start
  7.2 0.7 all-gather.2.cloned.1.call-update
  7.9 0.0 all-reduce.4.cloned.1.call-start
  8.0 0.7 convert_element_type.70
  8.7 1.4 convert_reduce_fusion.1
  10.0 1.3 pad_maximum_fusion.1
  11.3 0.1 fusion.32
  11.4 0.1 fusion.31
  11.5 0.8 constant_dynamic-update-slice_fusion
  12.4 8.8 %fusion.4 = bf16[4,128,2,128]{3,2,1,0:T(2,128)(2,1)} fusion(bf16[4,128,128,128]{3,2,1,0:T(8,128)(2,1)} %param.11, f32[128,2]{0,1:T(2,128)S(1)} %fusion.31), kind=kOutput, calls=%fused_computation.11 | convolution fusion | flops 33685760 | bytes 17040384 | tf_op jit(solution)/shard_map/wijd,js->wisd/dot_general | solution.py:39
  21.1 47.3 %all-gather.2.cloned.1.call-done = bf16[4,512,256]{2,1,0:T(8,128)(2,1)} async-done(((bf16[4,32,256]{2,1,0:T(8,128)(2,1)}), bf16[4,512,256]{2,1,0:T(8,128)(2,1)}) %all-gather.2.cloned.1.call-update) | async-done | bytes 1048592 | tf_op jit(solution)/shard_map/all_gather | solution.py:33
  68.4 1.2 fusion.12
  69.7 33.3 %add_convert_fusion = (bf16[4,128,128,128]{3,2,1,0:T(8,128)(2,1)}, f32[4,128,128]{2,1,0:T(8,128)S(1)}, f32[4,128,128,128]{3,2,1,0:T(8,128)}) fusion(bf16[4,128,128,128]{3,2,1,0:T(8,128)(2,1)} %param.11, f32[128]{0:T(128)} %param.17, f32[4,128,128]{2,1,0:T(8,128)S(1)} %fusion.12, bf16[4,128,128,128]{3,2,1,0:T(8,128)(2,1)} %param.19, bf16[128,128]{1,0:T(8,128)(2,1)} %param.15), kind=kOutput, calls=%fused_computation.6 | convolution fusion | flops 2248081408 | bytes 84443648 | tf_op jit(solution)/shard_map/wijd,de->wije/dot_general | solution.py:62
  102.9 1.1 fusion.3
  104.0 0.0 all-reduce.4.cloned.1.call-update
  104.1 0.0 all-reduce.6.cloned.1.call-start
  104.1 0.2 fusion.6
  104.4 34.3 %all-reduce.4.cloned.1.call-done = bf16[4,128,256]{2,1,0:T(8,128)(2,1)} async-done(((bf16[4,128,256]{2,1,0:T(8,128)(2,1)}), bf16[4,128,256]{2,1,0:T(8,128)(2,1)}) %all-reduce.4.cloned.1.call-update) | async-done | bytes 262160 | tf_op jit(solution)/shard_map/psum | solution.py:96
  138.7 1.7 broadcast_select_fusion
  140.4 0.0 all-reduce.6.cloned.1.call-update
  140.4 47.2 %all-reduce.6.cloned.1.call-done = (bf16[4,128,2,128]{3,2,1,0:T(2,128)(2,1)}, bf16[4,128,256]{2,1,0:T(8,128)(2,1)}) async-done(((bf16[4,128,2,128]{3,2,1,0:T(2,128)(2,1)}, bf16[4,128,256]{2,1,0:T(8,128)(2,1)}), (bf16[4,128,2,128]{3,2,1,0:T(2,128)(2,1)}, bf16[4,128,256]{2,1,0:T(8,128)(2,1)})) %all-reduce.6.cloned.1.call-update) | async-done | bytes 524304 | tf_op jit(solution)/shard_map/psum | solution.py:42
  187.6 1.0 fusion.16
  188.5 0.1 fusion.39
  188.7 0.9 add_convert_fusion.1
  189.6 0.3 fusion.7
  190.0 41.3 %psum.29 = f32[4,2,256]{2,0,1:T(4,128)S(1)} all-reduce(f32[4,2,256]{2,0,1:T(4,128)S(1)} %bitcast.78), channel_id=1, replica_groups=mesh['row'=4,'col'=4,'walk'=2] {'row','col'}, use_global_device_ids=true, to_apply=%region_4.0 | all-reduce | flops 2048 | bytes 16384 | tf_op jit(solution)/shard_map/psum | solution.py:101
  231.3 1.3 fusion.27
  232.5 7.7 %all_gather.7 = bf16[4,128,2,128]{3,1,0,2:T(8,128)(2,1)S(1)} all-gather(bf16[4,32,2,128]{3,1,0,2:T(8,128)(2,1)S(1)} %copy_bitcast_fusion), channel_id=1, replica_groups=mesh['row'=4,'col'=4,'walk'=2] {'col'}, dimensions={1}, use_global_device_ids=true | all-gather | bytes 327680 | tf_op jit(solution)/shard_map/all_gather | solution.py:77
  240.2 1.3 fusion.11
  241.6 1.6 fusion.15
  243.2 35.0 %fusion.2 = bf16[4,128,128,128]{3,2,1,0:T(8,128)(2,1)} fusion(bf16[4,128,128,128]{3,2,1,0:T(8,128)(2,1)} %param.19, f32[4,128,128]{2,1,0:T(8,128)S(1)} %get-tuple-element.11, f32[128]{0:T(128)S(1)} %get-tuple-element.20, f32[4,128,128]{2,1,0:T(8,128)S(1)} %get-tuple-element.10, f32[128]{0:T(128)S(1)} %get-tuple-element.19, ...), kind=kOutput, calls=%fused_computation.4 | convolution fusion | flops 2273312768 | bytes 67929600 | tf_op jit(solution)/shard_map/wije,de->wijd/dot_general | solution.py:87
  (26 shorter events, 0.2 us)
Async XLA Ops:
  7.2 181.5 %copy-start = (bf16[1024,256]{1,0:T(8,128)(2,1)S(1)}, bf16[1024,256]{1,0:T(8,128)(2,1)}, u32[]{:S(2)}) copy-start(bf16[1024,256]{1,0:T(8,128)(2,1)} %param.13) | copy-start | bytes 1572868
  7.2 61.2 %all-gather.2.cloned.1.call-start = ((), (), s32[]{:S(2)}) async-start(), calls=%async_computation | async-start | bytes 1114112 | tf_op jit(solution)/shard_map/all_gather | solution.py:33
  7.9 130.8 %all-reduce.4.cloned.1.call-start = ((), (), s32[]{:S(2)}) async-start(), calls=%async_computation.1 | async-start | bytes 524288 | tf_op jit(solution)/shard_map/psum | solution.py:96
  69.6 33.4 %copy-start.4 = (bf16[256,128]{1,0:T(8,128)(2,1)S(1)}, bf16[256,128]{1,0:T(8,128)(2,1)}, u32[]{:S(2)}) copy-start(bf16[256,128]{1,0:T(8,128)(2,1)} %param.16) | copy-start | bytes 196612
  69.6 34.5 %copy-start.1 = (bf16[4,512,256]{2,1,0:T(8,128)(2,1)S(1)}, bf16[4,512,256]{2,1,0:T(8,128)(2,1)}, u32[]{:S(2)}) copy-start(bf16[4,512,256]{2,1,0:T(8,128)(2,1)} %all-gather.2.cloned.1.call-done) | copy-start | bytes 3145732
  69.6 119.1 %copy-start.2 = (bf16[4,32,256]{2,1,0:T(8,128)(2,1)S(1)}, bf16[4,32,256]{2,1,0:T(8,128)(2,1)}, u32[]{:S(2)}) copy-start(bf16[4,32,256]{2,1,0:T(8,128)(2,1)} %param.10) | copy-start | bytes 196612
  69.6 119.1 %copy-start.5 = (f32[256]{0:T(256)S(1)}, f32[256]{0:T(256)}, u32[]{:S(2)}) copy-start(f32[256]{0:T(256)} %param.14) | copy-start | bytes 3076
  69.6 120.0 %copy-start.3 = (bf16[4,32,256]{2,1,0:T(8,128)(2,1)S(1)}, bf16[4,32,256]{2,1,0:T(8,128)(2,1)}, u32[]{:S(2)}) copy-start(bf16[4,32,256]{2,1,0:T(8,128)(2,1)} %param.18) | copy-start | bytes 196612
  69.6 173.5 %copy-start.6 = (bf16[128,128]{1,0:T(8,128)(2,1)S(1)}, bf16[128,128]{1,0:T(8,128)(2,1)}, u32[]{:S(2)}) copy-start(bf16[128,128]{1,0:T(8,128)(2,1)} %param.15) | copy-start | bytes 98308
  69.6 173.5 %copy-start.7 = (f32[128]{0:T(128)S(1)}, f32[128]{0:T(128)}, u32[]{:S(2)}) copy-start(f32[128]{0:T(128)} %param.17) | copy-start | bytes 1540
  104.1 83.5 %all-reduce.6.cloned.1.call-start = ((), (), s32[]{:S(2)}) async-start(), calls=%async_computation.2 | async-start | bytes 1048576 | tf_op jit(solution)/shard_map/psum | solution.py:42
Sparse Core Ops, SparseCore 0:
  10.7 57.6 all-gather.1
  104.2 34.4 all-reduce.3
  142.3 45.2 all-reduce.5
where the time goes:
time: 285 us
  waiting for transfers between devices  129 us (45%)
  matrix products  80.7 us (28%)
  blocking collectives  48.9 us (17%)
  between operations  14 us (5%)
  other arithmetic  10.4 us (4%)
    all_gather x1, waiting for transfers between devices, body(): everyone = lax.all_gather(one_elec, ('row', 'col'), axis=1, tiled=True)  47.3 us
    psum x1, waiting for transfers between devices, body(): lax.psum(partial_value.astype(jnp.bfloat16), 'col').astype(jnp.float32)  47.2 us
    psum x1, blocking collectives, body(): mean_total = lax.psum(mean_sums, ('row', 'col'))  41.3 us
    dot_general x1, matrix products, body(): jnp.einsum('wije,de->wijd', pair_delta, w_pair, preferred_element_type=jn...  35 us
    psum x1, waiting for transfers between devices, body(): lax.psum(message_grad.astype(jnp.bfloat16), 'row').astype(jnp.float32)  34.3 us
    dot_general x1, matrix products, body(): jnp.einsum('wijd,de->wije', pair, w_pair, preferred_element_type=jnp.floa...  33.3 us
    dot_general x1, matrix products, body(): jnp.einsum('wijd,js->wisd', pair, col_table.astype(jnp.bfloat16), preferr...  8.75 us
    all_gather x1, blocking collectives, body(): lax.all_gather(grad_pair_means.astype(jnp.bfloat16), 'col', axis=1, tiled...  7.66 us
  transfers between devices with their start and end apart: 3, of which 3 were waited for; matrix products, arithmetic and copies ran while one was open for 5% of the time, Pallas kernels for 0%

commit v1 on v0

--- a/solution.py
+++ b/solution.py
@@ -98,7 +98,7 @@
         column_total.dtype
     )
     own_message = lax.dynamic_slice_in_dim(row_total, col_index * own_rows, own_rows, 1)
-    mean_total = lax.psum(mean_sums, ("row", "col"))
+    mean_total = jnp.sum(lax.all_gather(mean_sums, ("row", "col")), axis=0)
     own_up = own_table[:, 0]
     own_down = own_table[:, 1]
     electron_grad = (

time: 285 us -> 284 us (level)
    psum x1 -> x0, blocking collectives: 41.3 us -> none  [body(): mean_total = lax.psum(mean_sums, ('row', 'col'))]
    all_gather x0 -> x1, blocking collectives: none -> 40.4 us  [body(): mean_total = jnp.sum(lax.all_gather(mean_sums, ('row', 'col')), axis=0)]
where the time goes in v1:
time: 284 us
  waiting for transfers between devices  129 us (45%)
  matrix products  80.7 us (28%)
  blocking collectives  48 us (17%)
  between operations  14 us (5%)
  other arithmetic  10.4 us (4%)
    all_gather x1, waiting for transfers between devices, body(): everyone = lax.all_gather(one_elec, ('row', 'col'), axis=1, tiled=True)  47.3 us
    psum x1, waiting for transfers between devices, body(): lax.psum(partial_value.astype(jnp.bfloat16), 'col').astype(jnp.float32)  47.2 us
    all_gather x1, blocking collectives, body(): mean_total = jnp.sum(lax.all_gather(mean_sums, ('row', 'col')), axis=0)  40.4 us
    dot_general x1, matrix products, body(): jnp.einsum('wije,de->wijd', pair_delta, w_pair, preferred_element_type=jn...  35 us
    psum x1, waiting for transfers between devices, body(): lax.psum(message_grad.astype(jnp.bfloat16), 'row').astype(jnp.float32)  34.3 us
    dot_general x1, matrix products, body(): jnp.einsum('wijd,de->wije', pair, w_pair, preferred_element_type=jnp.floa...  33.3 us
    dot_general x1, matrix products, body(): jnp.einsum('wijd,js->wisd', pair, col_table.astype(jnp.bfloat16), preferr...  8.75 us
    all_gather x1, blocking collectives, body(): lax.all_gather(grad_pair_means.astype(jnp.bfloat16), 'col', axis=1, tiled...  7.66 us
  transfers between devices with their start and end apart: 3, of which 3 were waited for; matrix products, arithmetic and copies ran while one was open for 5% of the time, Pallas kernels for 0%

profile of v1, /device:TPU:0, one launch (start us, length us, event | category | flops | bytes accessed | tf_op | source)
XLA Modules:
  0.0 283.8 jit_solution(6116458091535966705)
XLA Ops:
  7.2 0.0 copy-start
  7.2 0.0 all-gather.2.cloned.1.call-start
  7.2 0.7 all-gather.2.cloned.1.call-update
  7.9 0.0 all-reduce.4.cloned.1.call-start
  8.0 0.7 convert_element_type.70
  8.7 1.4 convert_reduce_fusion.1
  10.0 1.3 pad_maximum_fusion.1
  11.3 0.1 fusion.32
  11.4 0.1 fusion.31
  11.5 0.8 constant_dynamic-update-slice_fusion
  12.4 8.8 %fusion.4 = bf16[4,128,2,128]{3,2,1,0:T(2,128)(2,1)} fusion(bf16[4,128,128,128]{3,2,1,0:T(8,128)(2,1)} %param.11, f32[128,2]{0,1:T(2,128)S(1)} %fusion.31), kind=kOutput, calls=%fused_computation.11 | convolution fusion | flops 33685760 | bytes 17040384 | tf_op jit(solution)/shard_map/wijd,js->wisd/dot_general | solution.py:39
  21.1 47.3 %all-gather.2.cloned.1.call-done = bf16[4,512,256]{2,1,0:T(8,128)(2,1)} async-done(((bf16[4,32,256]{2,1,0:T(8,128)(2,1)}), bf16[4,512,256]{2,1,0:T(8,128)(2,1)}) %all-gather.2.cloned.1.call-update) | async-done | bytes 1048592 | tf_op jit(solution)/shard_map/all_gather | solution.py:33
  68.4 1.2 fusion.12
  69.7 33.3 %add_convert_fusion = (bf16[4,128,128,128]{3,2,1,0:T(8,128)(2,1)}, f32[4,128,128]{2,1,0:T(8,128)S(1)}, f32[4,128,128,128]{3,2,1,0:T(8,128)}) fusion(bf16[4,128,128,128]{3,2,1,0:T(8,128)(2,1)} %param.11, f32[128]{0:T(128)} %param.17, f32[4,128,128]{2,1,0:T(8,128)S(1)} %fusion.12, bf16[4,128,128,128]{3,2,1,0:T(8,128)(2,1)} %param.19, bf16[128,128]{1,0:T(8,128)(2,1)} %param.15), kind=kOutput, calls=%fused_computation.6 | convolution fusion | flops 2248081408 | bytes 84443648 | tf_op jit(solution)/shard_map/wijd,de->wije/dot_general | solution.py:62
  102.9 1.1 fusion.3
  104.0 0.0 all-reduce.4.cloned.1.call-update
  104.1 0.0 all-reduce.6.cloned.1.call-start
  104.1 0.2 fusion.6
  104.4 34.3 %all-reduce.4.cloned.1.call-done = bf16[4,128,256]{2,1,0:T(8,128)(2,1)} async-done(((bf16[4,128,256]{2,1,0:T(8,128)(2,1)}), bf16[4,128,256]{2,1,0:T(8,128)(2,1)}) %all-reduce.4.cloned.1.call-update) | async-done | bytes 262160 | tf_op jit(solution)/shard_map/psum | solution.py:96
  138.7 1.7 broadcast_select_fusion
  140.4 0.0 all-reduce.6.cloned.1.call-update
  140.4 47.2 %all-reduce.6.cloned.1.call-done = (bf16[4,128,2,128]{3,2,1,0:T(2,128)(2,1)}, bf16[4,128,256]{2,1,0:T(8,128)(2,1)}) async-done(((bf16[4,128,2,128]{3,2,1,0:T(2,128)(2,1)}, bf16[4,128,256]{2,1,0:T(8,128)(2,1)}), (bf16[4,128,2,128]{3,2,1,0:T(2,128)(2,1)}, bf16[4,128,256]{2,1,0:T(8,128)(2,1)})) %all-reduce.6.cloned.1.call-update) | async-done | bytes 524304 | tf_op jit(solution)/shard_map/psum | solution.py:42
  187.6 1.0 fusion.16
  188.5 0.1 fusion.39
  188.7 0.9 add_convert_fusion.1
  189.6 0.3 fusion.7
  190.0 40.4 %all_gather.14 = f32[16,4,2,256]{3,1,2,0:T(4,128)S(1)} all-gather(f32[1,4,2,256]{3,1,2,0:T(4,128)S(1)} %bitcast.78), channel_id=1, replica_groups=mesh['row'=4,'col'=4,'walk'=2] {'row','col'}, dimensions={0}, use_global_device_ids=true | all-gather | bytes 139264 | tf_op jit(solution)/shard_map/all_gather | solution.py:101
  230.4 1.3 fusion.27
  231.6 7.7 %all_gather.15 = bf16[4,128,2,128]{3,1,0,2:T(8,128)(2,1)S(1)} all-gather(bf16[4,32,2,128]{3,1,0,2:T(8,128)(2,1)S(1)} %copy_bitcast_fusion), channel_id=1, replica_groups=mesh['row'=4,'col'=4,'walk'=2] {'col'}, dimensions={1}, use_global_device_ids=true | all-gather | bytes 327680 | tf_op jit(solution)/shard_map/all_gather | solution.py:77
  239.3 1.3 fusion.11
  240.7 1.6 fusion.15
  242.3 35.0 %fusion.2 = bf16[4,128,128,128]{3,2,1,0:T(8,128)(2,1)} fusion(bf16[4,128,128,128]{3,2,1,0:T(8,128)(2,1)} %param.19, f32[4,128,128]{2,1,0:T(8,128)S(1)} %get-tuple-element.11, f32[128]{0:T(128)S(1)} %get-tuple-element.20, f32[4,128,128]{2,1,0:T(8,128)S(1)} %get-tuple-element.10, f32[128]{0:T(128)S(1)} %get-tuple-element.19, ...), kind=kOutput, calls=%fused_computation.4 | convolution fusion | flops 2273312768 | bytes 67929600 | tf_op jit(solution)/shard_map/wije,de->wijd/dot_general | solution.py:87
  (27 shorter events, 0.2 us)
Async XLA Ops:
  7.2 181.5 %copy-start = (bf16[1024,256]{1,0:T(8,128)(2,1)S(1)}, bf16[1024,256]{1,0:T(8,128)(2,1)}, u32[]{:S(2)}) copy-start(bf16[1024,256]{1,0:T(8,128)(2,1)} %param.13) | copy-start | bytes 1572868
  7.2 61.2 %all-gather.2.cloned.1.call-start = ((), (), s32[]{:S(2)}) async-start(), calls=%async_computation | async-start | bytes 1114112 | tf_op jit(solution)/shard_map/all_gather | solution.py:33
  7.9 130.8 %all-reduce.4.cloned.1.call-start = ((), (), s32[]{:S(2)}) async-start(), calls=%async_computation.1 | async-start | bytes 524288 | tf_op jit(solution)/shard_map/psum | solution.py:96
  69.6 33.4 %copy-start.4 = (bf16[256,128]{1,0:T(8,128)(2,1)S(1)}, bf16[256,128]{1,0:T(8,128)(2,1)}, u32[]{:S(2)}) copy-start(bf16[256,128]{1,0:T(8,128)(2,1)} %param.16) | copy-start | bytes 196612
  69.6 34.5 %copy-start.1 = (bf16[4,512,256]{2,1,0:T(8,128)(2,1)S(1)}, bf16[4,512,256]{2,1,0:T(8,128)(2,1)}, u32[]{:S(2)}) copy-start(bf16[4,512,256]{2,1,0:T(8,128)(2,1)} %all-gather.2.cloned.1.call-done) | copy-start | bytes 3145732
  69.6 119.1 %copy-start.2 = (bf16[4,32,256]{2,1,0:T(8,128)(2,1)S(1)}, bf16[4,32,256]{2,1,0:T(8,128)(2,1)}, u32[]{:S(2)}) copy-start(bf16[4,32,256]{2,1,0:T(8,128)(2,1)} %param.10) | copy-start | bytes 196612
  69.6 119.1 %copy-start.5 = (f32[256]{0:T(256)S(1)}, f32[256]{0:T(256)}, u32[]{:S(2)}) copy-start(f32[256]{0:T(256)} %param.14) | copy-start | bytes 3076
  69.6 120.0 %copy-start.3 = (bf16[4,32,256]{2,1,0:T(8,128)(2,1)S(1)}, bf16[4,32,256]{2,1,0:T(8,128)(2,1)}, u32[]{:S(2)}) copy-start(bf16[4,32,256]{2,1,0:T(8,128)(2,1)} %param.18) | copy-start | bytes 196612
  69.6 172.6 %copy-start.6 = (bf16[128,128]{1,0:T(8,128)(2,1)S(1)}, bf16[128,128]{1,0:T(8,128)(2,1)}, u32[]{:S(2)}) copy-start(bf16[128,128]{1,0:T(8,128)(2,1)} %param.15) | copy-start | bytes 98308
  69.6 172.6 %copy-start.7 = (f32[128]{0:T(128)S(1)}, f32[128]{0:T(128)}, u32[]{:S(2)}) copy-start(f32[128]{0:T(128)} %param.17) | copy-start | bytes 1540
  104.1 83.5 %all-reduce.6.cloned.1.call-start = ((), (), s32[]{:S(2)}) async-start(), calls=%async_computation.2 | async-start | bytes 1048576 | tf_op jit(solution)/shard_map/psum | solution.py:42
Sparse Core Ops, SparseCore 0:
  10.7 57.6 all-gather.1
  104.2 34.4 all-reduce.3
  142.3 45.2 all-reduce.5
